TPU v7x, 32 devices: a whole 2x2x4 slice. The times are simulated.
32 devices in a mesh: vis: 2 (over x), ctx: 8 (over z, y), tp: 2 (over core).
Axes of the slice: x: 2, y: 2, z: 4, core: 2. Of those that a mesh axis runs over, the one named last changes fastest.
Arguments:
- patch_rows: bfloat16 [1024, 1280], P('ctx'), may hold values from -6 to 6
- vit_gain: float32 [1280], replicated, may hold values from 0.25 to 1.75
- vit_bias: float32 [1280], replicated, may hold values from -3 to 3
- vit_qkv: bfloat16 [1280, 3, 16, 80], P(None, None, ('vis', 'tp')), as said below
- vit_out: bfloat16 [16, 80, 1280], P(('vis', 'tp')), may hold values from -0.15625 to 0.15625
- merge_gain: float32 [1280], replicated, may hold values from 0.25 to 1.75
- merge_bias: float32 [1280], replicated, may hold values from -3 to 3
- merge_weight: bfloat16 [5120, 4096], P('ctx', ('vis', 'tp')), may hold values from -0.078125 to 0.078125
- image_patches: int32 [8, 2], replicated, may hold values from 4 to 64, as said below
- window_ids: int32 [1024], P('ctx'), may hold values from 0 to 1023, as said below
- image_pos: int32 [256], replicated, may hold values from 0 to 1023, as said below
- slice_order: int32 [8], replicated, may hold values from 0 to 7, as said below
- doc_ids: int32 [1024], replicated, may hold values from 0 to 3, never falling along the last dimension, each value on 1 to 512 neighbouring positions
- text_rows: bfloat16 [1024, 4096], P('ctx', ('vis', 'tp')), may hold values from -6 to 6
- norm_gain: float32 [4096], replicated, may hold values from 0.25 to 1.75
- w_query: bfloat16 [4096, 8, 4, 128], P(None, 'vis', 'tp'), as said below
- w_keyval: bfloat16 [2, 4096, 8, 128], P('tp', None, 'vis'), as said below
Outputs:
- attention_out: bfloat16 [1024, 8, 512], P('ctx', 'vis', 'tp')
Inputs may be any that keep to these rules, and one draw needn't show every extreme that they name: `image_patches`: each is h * w for an image of h by w patches, h and w even and at most 32; the images of one ctx shard hold at most 128 patches together, exactly 128 on some shard. `window_ids`: equal ids mark one attention window: consecutive slots of one ctx shard, a multiple of 4 of them and at most 64, never in two images; slots after a shard's live patches form windows of 4. `slice_order`: a permutation; ctx shard c holds the sequence slices slice_order[c] and 15 - slice_order[c] of 64 positions, in that order, as its 128 rows. `image_pos`: distinct positions, one for every merged slot, live or not; the 32 slots of any one ctx shard put exactly 4 positions into the rows of each ctx shard. `doc_ids`: never falling along positions; each document holds 1 to 512 positions. `vit_qkv`: independent centred entries. `w_query`: independent centred entries. `w_keyval`: independent centred entries.
All inputs are finite; a program needn't handle non-finite values.
Results may differ from a plain program's by a relative error of at most 0.022.
The roundings to bfloat16 on the way count: a program that leaves them out, or rounds other values in their place, can miss the bound.
Values may be sent and summed in bfloat16 or wider, within the bound.
No kernel may reach another device: no remote copies, remote signals or barrier semaphores. Data moves between devices by JAX's collectives and lax.ppermute only.
A program may use at most 64 MiB of HBM per device.

v0:
```python
import math
import jax
import jax.numpy as jnp
from jax import lax
from jax.sharding import PartitionSpec as P

D = 4096
HD = 128
VD = 1280
VHD = 80
TOK = 128
PCAP = 128
ICAP = 32
norm_eps = 1e-06
rope_base = 1000000.0
big_negative = -1e30


def swapped(value, axis, stride):
    return lax.ppermute(value, axis, [(i, i ^ 1 << stride) for i in range(lax.axis_size(axis))])


def layer_norm(values, scale_vec, shift_vec):
    centre = jnp.mean(values, axis=-1, keepdims=True)
    offset = values - centre
    spread = jnp.mean(offset * offset, axis=-1, keepdims=True)
    return offset * lax.rsqrt(spread + norm_eps) * scale_vec + shift_vec


def rotate(values, positions):
    half_dim = values.shape[-1] // 2
    exponent = jnp.arange(half_dim, dtype=jnp.float32) * (-2.0 / values.shape[-1])
    frequency = jnp.power(jnp.float32(rope_base), exponent)
    angles = positions.astype(jnp.float32)[:, None] * frequency[None, :]
    shape_out = (values.shape[0],) + (1,) * (values.ndim - 2) + (half_dim,)
    cosine = jnp.cos(angles).reshape(shape_out)
    sine_part = jnp.sin(angles).reshape(shape_out)
    lead_half = values[..., :half_dim]
    tail_half = values[..., half_dim:]
    return jnp.concatenate(
        [lead_half * cosine - tail_half * sine_part, tail_half * cosine + lead_half * sine_part],
        axis=-1,
    )


def row_positions(row_ids, slice_order, tokens_dev):
    shards = slice_order.shape[0]
    device_of = row_ids // tokens_dev
    local_row = row_ids % tokens_dev
    half_tok = tokens_dev // 2
    matches = device_of[:, None] == jnp.arange(shards, dtype=jnp.int32)[None, :]
    first_slice = jnp.sum(jnp.where(matches, slice_order[None, :], 0), axis=1)
    slice_ids = jnp.where(local_row < half_tok, first_slice, 2 * shards - 1 - first_slice)
    return slice_ids * half_tok + local_row % half_tok


def place_of(positions, slice_order, tokens_dev):
    shards = slice_order.shape[0]
    half_tok = tokens_dev // 2
    slice_ids = positions // half_tok
    paired = jnp.minimum(slice_ids, 2 * shards - 1 - slice_ids)
    owner_hot = (paired[..., None] == slice_order).astype(jnp.int32)
    owner_dev = jnp.sum(owner_hot * jnp.arange(shards, dtype=jnp.int32), axis=-1)
    local_row = jnp.where(slice_ids < shards, 0, half_tok) + positions % half_tok
    return (owner_dev, local_row, owner_hot)


def local(
    patch_rows,
    vit_gain,
    vit_bias,
    vit_qkv,
    vit_out,
    merge_gain,
    merge_bias,
    merge_weight,
    image_patches,
    window_ids,
    image_pos,
    slice_order,
    doc_ids,
    text_rows,
    norm_gain,
    w_query,
    w_keyval,
):
    shards = lax.axis_size("ctx")
    ctx_index = lax.axis_index("ctx")
    tp_index = lax.axis_index("tp")
    vit_heads = vit_qkv.shape[2]
    slab_width = merge_weight.shape[1]
    normed = layer_norm(patch_rows.astype(jnp.float32), vit_gain, vit_bias).astype(jnp.bfloat16)
    projected = jnp.dot(
        normed, vit_qkv.reshape(VD, 3 * vit_heads * VHD), preferred_element_type=jnp.float32
    )
    projected = projected.astype(jnp.bfloat16).reshape(PCAP, 3, vit_heads, VHD)
    scores = jnp.einsum(
        "qhd,khd->hqk", projected[:, 0], projected[:, 1], preferred_element_type=jnp.float32
    ) / math.sqrt(VHD)
    allowed = window_ids[:, None] == window_ids[None, :]
    scores = jnp.where(allowed[None], scores, big_negative)
    powers = jnp.exp(scores - jnp.max(scores, axis=-1, keepdims=True))
    totals = jnp.sum(powers, axis=-1)
    blended = jnp.einsum(
        "hqk,khd->qhd",
        powers.astype(jnp.bfloat16),
        projected[:, 2],
        preferred_element_type=jnp.float32,
    )
    blended = (
        (blended / jnp.transpose(totals)[:, :, None])
        .astype(jnp.bfloat16)
        .reshape(PCAP, vit_heads * VHD)
    )
    out_flat = vit_out.reshape(vit_heads * VHD, VD)
    branch_part = jnp.dot(blended, out_flat, preferred_element_type=jnp.float32)
    branch_sum = lax.psum(branch_part, ("vis", "tp"))
    hidden = patch_rows.astype(jnp.float32) + branch_sum
    merged = layer_norm(hidden, merge_gain, merge_bias).astype(jnp.bfloat16).reshape(ICAP, 4 * VD)
    image_emb = jnp.dot(
        merged,
        lax.all_gather(merge_weight, "ctx", axis=0, tiled=True),
        preferred_element_type=jnp.float32,
    ).astype(jnp.bfloat16)
    send_each = ICAP // shards
    slot_ids = jnp.arange(ICAP, dtype=jnp.int32)
    shard_ids = jnp.arange(shards, dtype=jnp.int32)
    live_count = jnp.sum(image_patches, axis=1) // 4
    all_pos = image_pos.reshape(shards, ICAP)
    owner_dev, local_row, owner_hot = place_of(all_pos, slice_order, TOK)
    before = jnp.cumsum(owner_hot, axis=1) - owner_hot
    rank_in = jnp.sum(before * owner_hot, axis=-1)
    is_live = slot_ids[None, :] < live_count[:, None]
    own_hot = (shard_ids == ctx_index)[:, None]
    own_owner = jnp.sum(jnp.where(own_hot, owner_dev, 0), axis=0)
    own_rank = jnp.sum(jnp.where(own_hot, rank_in, 0), axis=0)
    own_live = jnp.any(own_hot & is_live, axis=0)
    target_slot = own_owner * send_each + own_rank
    picker = ((target_slot[None, :] == slot_ids[:, None]) & own_live[None, :]).astype(jnp.bfloat16)
    outgoing = jnp.dot(picker, image_emb, preferred_element_type=jnp.float32).astype(jnp.bfloat16)
    incoming = lax.all_to_all(
        outgoing.reshape(shards, send_each, slab_width),
        "ctx",
        split_axis=0,
        concat_axis=0,
        tiled=True,
    )
    mine_live = ((owner_dev == ctx_index) & is_live).reshape(-1)
    column_of = (shard_ids[:, None] * send_each + rank_in).reshape(-1)
    row_hot = (
        (local_row.reshape(-1)[None, :] == jnp.arange(TOK, dtype=jnp.int32)[:, None])
        & mine_live[None, :]
    ).astype(jnp.bfloat16)
    column_hot = (column_of[:, None] == slot_ids[None, :]).astype(jnp.bfloat16)
    placing = jnp.dot(row_hot, column_hot, preferred_element_type=jnp.float32)
    is_image = jnp.sum(placing, axis=1) > 0.5
    image_part = jnp.dot(
        placing.astype(jnp.bfloat16),
        incoming.reshape(ICAP, slab_width),
        preferred_element_type=jnp.float32,
    )
    embeds = jnp.where(is_image[:, None], image_part.astype(jnp.bfloat16), text_rows)
    full_rows = lax.all_gather(embeds, ("vis", "tp"), axis=1, tiled=True)
    widened = full_rows.astype(jnp.float32)
    normed_rows = (
        widened
        * lax.rsqrt(jnp.mean(widened * widened, axis=1, keepdims=True) + norm_eps)
        * norm_gain
    ).astype(jnp.bfloat16)
    own_positions = row_positions(
        ctx_index * TOK + jnp.arange(TOK, dtype=jnp.int32), slice_order, TOK
    )
    own_doc = jnp.take(doc_ids, own_positions)
    kv_heads = w_query.shape[1]
    groups = w_query.shape[2]
    queries = jnp.dot(
        normed_rows, w_query.reshape(D, kv_heads * groups * HD), preferred_element_type=jnp.float32
    ).reshape(TOK, kv_heads, groups, HD)
    queries = rotate(queries, own_positions).astype(jnp.bfloat16)
    projected_half = jnp.dot(
        normed_rows, w_keyval[0].reshape(D, kv_heads * HD), preferred_element_type=jnp.float32
    ).reshape(TOK, kv_heads, HD)
    own_half = jnp.where(
        tp_index == 0, rotate(projected_half, own_positions), projected_half
    ).astype(jnp.bfloat16)
    initial = (
        jnp.full((kv_heads, groups, TOK), big_negative, jnp.float32),
        jnp.zeros((kv_heads, groups, TOK), jnp.float32),
        jnp.zeros((kv_heads, groups, TOK, HD), jnp.float32),
    )
    gathered = lax.all_gather(own_half, "ctx", axis=0, tiled=True)
    partner_all = swapped(gathered, "tp", 0)
    keys_every = jnp.where(tp_index == 0, gathered, partner_all)
    values_every = jnp.where(tp_index == 0, partner_all, gathered)
    carry_state = initial
    key_count = keys_every.shape[0]
    block_rows = key_count if key_count <= 1024 else math.gcd(key_count, 1024)
    block_count = key_count // block_rows
    key_pos = row_positions(jnp.arange(key_count, dtype=jnp.int32), slice_order, TOK)
    key_doc = jnp.take(doc_ids, key_pos)
    stacked = (
        keys_every.reshape(block_count, block_rows, kv_heads, HD),
        values_every.reshape(block_count, block_rows, kv_heads, HD),
        key_pos.reshape(block_count, block_rows),
        key_doc.reshape(block_count, block_rows),
    )

    def key_block(state_now, inputs_now):
        keys_blk, values_blk, pos_blk, doc_blk = inputs_now
        best_old, total_old, accum_old = state_now
        allowed_now = (pos_blk[None, :] <= own_positions[:, None]) & (
            doc_blk[None, :] == own_doc[:, None]
        )
        scores_now = jnp.einsum(
            "qkgd,nkd->kgqn", queries, keys_blk, preferred_element_type=jnp.float32
        ) / math.sqrt(HD)
        scores_now = jnp.where(allowed_now[None, None], scores_now, big_negative)
        best_new = jnp.maximum(best_old, jnp.max(scores_now, axis=-1))
        factor = jnp.exp(best_old - best_new)
        powers_now = jnp.where(
            allowed_now[None, None], jnp.exp(scores_now - best_new[..., None]), 0.0
        )
        total_new = total_old * factor + jnp.sum(powers_now, axis=-1)
        accum_new = accum_old * factor[..., None] + jnp.einsum(
            "kgqn,nkd->kgqd",
            powers_now.astype(jnp.bfloat16),
            values_blk,
            preferred_element_type=jnp.float32,
        )
        return ((best_new, total_new, accum_new), None)

    carry_state, unused = lax.scan(key_block, carry_state, stacked)
    best_final, total_final, accum_final = carry_state
    result = accum_final / total_final[..., None]
    return (
        jnp.transpose(result, (2, 0, 1, 3)).reshape(TOK, kv_heads, groups * HD).astype(jnp.bfloat16)
    )


def solution(mesh):
    placed = (
        P("ctx", None),
        P(),
        P(),
        P(None, None, ("vis", "tp"), None),
        P(("vis", "tp"), None, None),
        P(),
        P(),
        P("ctx", ("vis", "tp")),
        P(),
        P("ctx"),
        P(),
        P(),
        P(),
        P("ctx", ("vis", "tp")),
        P(),
        P(None, "vis", "tp", None),
        P("tp", None, "vis", None),
    )
    return jax.shard_map(
        local, mesh=mesh, in_specs=placed, out_specs=P("ctx", "vis", "tp"), check_vma=False
    )
```

profile of v0, /device:TPU:1, one launch (start us, length us, event | category | flops | bytes accessed | tf_op | source)
XLA Modules:
  0.0 267.5 jit_solution(11337003461193074470)
XLA Ops:
  7.4 1.2 convert_reduce_fusion
  8.7 1.3 fusion.43
  10.8 1.9 convolution_convert_fusion.1
  13.0 2.5 convolution_bitcast_fusion
  18.6 32.0 %all-reduce.2.cloned.1.call-done = f32[128,1280]{1,0:T(8,128)} async-done(((f32[128,1280]{1,0:T(8,128)}), f32[128,1280]{1,0:T(8,128)}) %all-reduce.2.cloned.1.call-update) | async-done | bytes 655376 | tf_op jit(solution)/shard_map/psum | solution.py:117
  50.5 1.2 fusion.58
  51.8 1.3 multiply_reduce_fusion
  53.1 1.3 add_convert_fusion
  54.6 114.9 %all-gather.4.cloned.1.call-done = bf16[5120,1024]{1,0:T(8,128)(2,1)} async-done(((bf16[640,1024]{1,0:T(8,128)(2,1)}), bf16[5120,1024]{1,0:T(8,128)(2,1)}) %all-gather.4.cloned.1.call-update) | async-done | bytes 10485776 | tf_op jit(solution)/shard_map/all_gather | solution.py:122
  169.5 6.1 %convolution_convert_fusion.2 = bf16[32,1024]{1,0:T(8,128)(2,1)S(1)} fusion(bf16[32,5120]{1,0:T(8,128)(2,1)S(1)} %reshape.660, bf16[5120,1024]{1,0:T(8,128)(2,1)} %all-gather.4.cloned.1.call-done, s32[32]{0:T(128)S(1)} %multiply_add_fusion.1, pred[32]{0:T(512)(128)(4,1)S(1)} %get-tuple-element.54), kind=kOutput, calls=%fused_computation.28 | convolution fusion | flops 337709056 | bytes 10879136 | tf_op jit(solution)/shard_map/dot_general | solution.py:140
  176.3 3.4 %all-to-all-start = ((bf16[8,4,1024]{2,1,0:T(4,128)(2,1)}), bf16[8,4,1024]{2,1,0:T(4,128)(2,1)S(1)}, u32[]{:S(2)}, u32[]{:S(2)}) async-start(bf16[8,4,1024]{2,1,0:T(4,128)(2,1)} %reshape.661), calls=%async_computation | async-start | bytes 131072 | tf_op jit(solution)/shard_map/all_to_all | solution.py:141
  179.7 5.6 %all-to-all-done = bf16[8,4,1024]{2,1,0:T(4,128)(2,1)S(1)} async-done(((bf16[8,4,1024]{2,1,0:T(4,128)(2,1)}), bf16[8,4,1024]{2,1,0:T(4,128)(2,1)S(1)}, u32[]{:S(2)}, u32[]{:S(2)}) %all-to-all-start) | async-done | bytes 65568 | tf_op jit(solution)/shard_map/all_to_all | solution.py:141
  188.2 4.9 %copy.79 = bf16[512,8,4,128]{3,1,2,0:T(8,128)(2,1)} copy(bf16[512,8,4,128]{3,2,1,0:T(4,128)(2,1)} %bitcast.116) | data formatting | bytes 8388608
  193.1 6.5 %copy.63 = bf16[512,4096]{1,0:T(8,128)(2,1)} copy(bf16[512,4096]{0,1:T(8,128)(2,1)} %bitcast.114) | data formatting | bytes 8388608 | tf_op jit(solution)/shard_map/dot_general | solution.py:180
  199.8 3.1 %all-gather.6.cloned.1.call-done = bf16[128,4096]{1,0:T(8,128)(2,1)} async-done(((bf16[128,1024]{1,0:T(8,128)(2,1)}), bf16[128,4096]{1,0:T(8,128)(2,1)}) %all-gather.6.cloned.1.call-update) | async-done | bytes 1048592 | tf_op jit(solution)/shard_map/all_gather | solution.py:163
  203.0 1.5 fusion.3
  204.5 3.8 %fusion.25 = f32[128,4,128]{0,2,1:T(8,128)S(1)} fusion(bf16[4,128,4096]{2,1,0:T(8,128)(2,1)} %bitcast.117, bf16[128,4096]{1,0:T(8,128)(2,1)} %all-gather.6.cloned.1.call-done, f32[4096]{0:T(1024)S(1)} %copy-done.14, f32[128]{0:T(128)S(1)} %add_rsqrt_fusion), kind=kOutput, calls=%fused_computation.35 | convolution fusion | flops 538968064 | bytes 5521920 | tf_op jit(solution)/shard_map/dot_general | solution.py:180
  209.3 4.5 %gather_fusion = s32[1024]{0:T(1024)S(1)} fusion(s32[1024]{0:T(1024)S(1)} %copy-done.1, s32[1024]{0:T(1024)S(1)} %broadcast_clamp_fusion), kind=kCustom, calls=%fused_computation | custom fusion | bytes 12288 | tf_op jit(solution)/shard_map/jit(_take)/gather | solution.py:200
  213.8 14.4 %reshape.663 = bf16[4096,1024]{1,0:T(8,128)(2,1)} reshape(bf16[4096,4,2,128]{3,2,1,0:T(2,128)(2,1)} %param.32) | data formatting | bytes 16777216 | tf_op jit(solution)/shard_map/reshape | solution.py:177
  228.2 11.4 %copy.64 = bf16[1024,4096]{1,0:T(8,128)(2,1)} copy(bf16[1024,4096]{0,1:T(8,128)(2,1)} %bitcast.113) | data formatting | bytes 16777216 | tf_op jit(solution)/shard_map/dot_general | solution.py:176
  239.5 6.1 %all-gather.8.cloned.1.call-done = bf16[1024,4,128]{0,2,1:T(8,128)(2,1)} async-done(((bf16[128,4,128]{0,2,1:T(8,128)(2,1)}), bf16[1024,4,128]{0,2,1:T(8,128)(2,1)}) %all-gather.8.cloned.1.call-update) | async-done | bytes 1048592 | tf_op jit(solution)/shard_map/all_gather | solution.py:191
  245.6 3.2 %collective-permute-start = (bf16[1024,4,128]{0,2,1:T(8,128)(2,1)}, bf16[1024,4,128]{0,2,1:T(8,128)(2,1)S(1)}, u32[]{:S(2)}, u32[]{:S(2)}) collective-permute-start(bf16[1024,4,128]{0,2,1:T(8,128)(2,1)} %all-gather.8.cloned.1.call-done), channel_id=1, source_target_pairs={{0,1},{1,0},{2,3},{3,2},{4,5},{5,4},{6,7},{7,6},{8,9},{9,8},{10,11... | collective-permute-start | bytes 3145736 | tf_op jit(solution)/shard_map/ppermute | solution.py:20
  249.8 5.9 %fusion.23 = f32[128,4,2,128]{0,3,2,1:T(8,128)S(1)} fusion(bf16[4,2,128,4096]{3,2,1,0:T(8,128)(2,1)} %bitcast.115, bf16[128,4096]{1,0:T(8,128)(2,1)S(1)} %copy-done.3, f32[4096]{0:T(1024)} %param.31, f32[128]{0:T(128)} %copy-done.15), kind=kOutput, calls=%fused_computation.33 | convolution fusion | flops 1075838976 | bytes 9978368 | tf_op jit(solution)/shard_map/dot_general | solution.py:176
  257.9 1.3 fusion.36
  (95 shorter events, 13.0 us)
Async XLA Ops:
  7.4 3.4 %copy-start = (bf16[1280,3,4,80]{0,3,2,1:T(8,128)(2,1)S(1)}, bf16[1280,3,4,80]{0,3,2,1:T(8,128)(2,1)}, u32[]{:S(2)}) copy-start(bf16[1280,3,4,80]{0,3,2,1:T(8,128)(2,1)} %param.20) | copy-start | bytes 7372804
  7.4 8.8 %copy-start.10 = (s32[256]{0:T(256)S(1)}, s32[256]{0:T(256)}, u32[]{:S(2)}) copy-start(s32[256]{0:T(256)} %param.27) | copy-start | bytes 3076
  7.4 9.0 %copy-start.9 = (s32[8]{0:T(128)S(1)}, s32[8]{0:T(128)}, u32[]{:S(2)}) copy-start(s32[8]{0:T(128)} %param.28) | copy-start | bytes 100
  7.4 43.2 %all-reduce.2.cloned.1.call-start = ((), (), s32[]{:S(2)}) async-start(), calls=%async_computation.1 | async-start | bytes 1310720 | tf_op jit(solution)/shard_map/psum | solution.py:117
  8.6 9.4 %copy-start.12 = (s32[8,2]{0,1:T(2,128)S(1)}, s32[8,2]{0,1:T(2,128)}, u32[]{:S(2)}) copy-start(s32[8,2]{0,1:T(2,128)} %param.25) | copy-start | bytes 196
  8.6 41.9 %copy-start.2 = (bf16[128,1280]{1,0:T(8,128)(2,1)S(1)}, bf16[128,1280]{1,0:T(8,128)(2,1)}, u32[]{:S(2)}) copy-start(bf16[128,1280]{1,0:T(8,128)(2,1)} %param.17) | copy-start | bytes 983044
  12.7 40.5 %copy-start.7 = (f32[1280]{0:T(1024)S(1)}, f32[1280]{0:T(1024)}, u32[]{:S(2)}) copy-start(f32[1280]{0:T(1024)} %param.23) | copy-start | bytes 15364
  12.7 40.5 %copy-start.8 = (f32[1280]{0:T(1024)S(1)}, f32[1280]{0:T(1024)}, u32[]{:S(2)}) copy-start(f32[1280]{0:T(1024)} %param.22) | copy-start | bytes 15364
  15.6 154.0 %all-gather.4.cloned.1.call-start = ((), (), s32[]{:S(2)}) async-start(), calls=%async_computation.2 | async-start | bytes 11796480 | tf_op jit(solution)/shard_map/all_gather | solution.py:122
  169.5 15.8 %copy-start.6 = (bf16[128,1024]{1,0:T(8,128)(2,1)S(1)}, bf16[128,1024]{1,0:T(8,128)(2,1)}, u32[]{:S(2)}) copy-start(bf16[128,1024]{1,0:T(8,128)(2,1)} %param.30) | copy-start | bytes 786436
  169.5 17.2 %copy-start.1 = (s32[1024]{0:T(1024)S(1)}, s32[1024]{0:T(1024)}, u32[]{:S(2)}) copy-start(s32[1024]{0:T(1024)} %param.29) | copy-start | bytes 12292
  176.3 9.1 %all-to-all-start = ((bf16[8,4,1024]{2,1,0:T(4,128)(2,1)}), bf16[8,4,1024]{2,1,0:T(4,128)(2,1)S(1)}, u32[]{:S(2)}, u32[]{:S(2)}) async-start(bf16[8,4,1024]{2,1,0:T(4,128)(2,1)} %reshape.661), calls=%async_computation | async-start | bytes 131072 | tf_op jit(solution)/shard_map/all_to_all | solution.py:141
  179.6 23.3 %all-gather.6.cloned.1.call-start = ((), (), s32[]{:S(2)}) async-start(), calls=%async_computation.3 | async-start | bytes 1310720 | tf_op jit(solution)/shard_map/all_gather | solution.py:163
  186.3 59.3 %all-gather.8.cloned.1.call-start = ((), (), s32[]{:S(2)}) async-start(), calls=%async_computation.4 | async-start | bytes 1179648 | tf_op jit(solution)/shard_map/all_gather | solution.py:191
  188.2 4.9 %copy-start.11 = (s32[128]{0:T(128)}, s32[128]{0:T(128)S(1)}, u32[]{:S(2)}) copy-start(s32[128]{0:T(128)S(1)} %get-tuple-element.30) | copy-start | bytes 1540
  193.1 11.4 %copy-start.14 = (f32[4096]{0:T(1024)S(1)}, f32[4096]{0:T(1024)}, u32[]{:S(2)}) copy-start(f32[4096]{0:T(1024)} %param.31) | copy-start | bytes 49156
  199.8 8.5 %copy-start.4 = (f32[128,64]{0,1:T(8,128)}, f32[128,64]{0,1:T(8,128)S(1)}, u32[]{:S(2)}) copy-start(f32[128,64]{0,1:T(8,128)S(1)} %get-tuple-element.52) | copy-start | bytes 98308
  204.5 4.6 %copy-start.15 = (f32[128]{0:T(128)}, f32[128]{0:T(128)S(1)}, u32[]{:S(2)}) copy-start(f32[128]{0:T(128)S(1)} %add_rsqrt_fusion) | copy-start | bytes 1540
  228.2 21.6 %copy-start.3 = (bf16[128,4096]{1,0:T(8,128)(2,1)S(1)}, bf16[128,4096]{1,0:T(8,128)(2,1)}, u32[]{:S(2)}) copy-start(bf16[128,4096]{1,0:T(8,128)(2,1)} %all-gather.6.cloned.1.call-done) | copy-start | bytes 3145732
  245.6 10.1 %collective-permute-start = (bf16[1024,4,128]{0,2,1:T(8,128)(2,1)}, bf16[1024,4,128]{0,2,1:T(8,128)(2,1)S(1)}, u32[]{:S(2)}, u32[]{:S(2)}) collective-permute-start(bf16[1024,4,128]{0,2,1:T(8,128)(2,1)} %all-gather.8.cloned.1.call-done), channel_id=1, source_target_pairs={{0,1},{1,0},{2,3},{3,2},{4,5},{5,4},{6,7},{7,6},{8,9},{9,8},{10,11... | collective-permute-start | bytes 3145736 | tf_op jit(solution)/shard_map/ppermute | solution.py:20
  249.8 5.9 %copy-start.5 = (f32[128,64]{0,1:T(8,128)S(1)}, f32[128,64]{0,1:T(8,128)}, u32[]{:S(2)}) copy-start(f32[128,64]{0,1:T(8,128)} %copy-done.4) | copy-start | bytes 98308
  249.8 6.0 %copy-start.13 = (bf16[1024,4,128]{0,2,1:T(8,128)(2,1)S(1)}, bf16[1024,4,128]{0,2,1:T(8,128)(2,1)}, u32[]{:S(2)}) copy-start(bf16[1024,4,128]{0,2,1:T(8,128)(2,1)} %all-gather.8.cloned.1.call-done) | copy-start | bytes 3145732
Sparse Core Ops, SparseCore 0:
  15.7 34.8 all-reduce.1
  186.5 16.4 all-gather.5
Sparse Core Ops, SparseCore 1:
  18.2 151.2 all-gather.3
  209.2 36.4 all-gather.7
where the time goes:
time: 269 us; the launch traced here: 267 us
  waiting for transfers between devices  162 us (60%)
  local copies, waits for them, and re-layouts  44.9 us (17%)
  matrix products  24 us (9%)
  between operations  15.2 us (6%)
  other arithmetic  14.2 us (5%)
  starting transfers between devices  6.82 us (3%)
    all_gather x1, waiting for transfers between devices, local(): lax.all_gather(merge_weight, 'ctx', axis=0, tiled=True)  115 us
    psum x1, waiting for transfers between devices, local(): branch_sum = lax.psum(branch_part, ('vis', 'tp'))  32 us
    reshape x1, local copies, waits for them, and re-layouts, local(): w_query.reshape(D, kv_heads * groups * HD)  14.4 us
    dot_general x1, local copies, waits for them, and re-layouts, local(): jnp.dot(normed_rows, w_query.reshape(D, kv_heads * groups * HD), preferre...  11.4 us
    dot_general x1, local copies, waits for them, and re-layouts, local(): jnp.dot(normed_rows, w_keyval[0].reshape(D, kv_heads * HD), preferred_ele...  6.52 us
    all_gather x1, waiting for transfers between devices, local(): gathered = lax.all_gather(own_half, 'ctx', axis=0, tiled=True)  6.11 us
    dot_general x1, matrix products, local(): jnp.dot(picker, image_emb, preferred_element_type=jnp.float32)  6.07 us
    dot_general x1, matrix products, local(): jnp.dot(normed_rows, w_query.reshape(D, kv_heads * groups * HD), preferre...  5.89 us
  transfers between devices with their start and end apart: 6, of which 5 were waited for; matrix products, arithmetic and copies ran while one was open for 21% of the time, Pallas kernels for 0%

commit v1 on v0

--- a/solution.py
+++ b/solution.py
@@ -14,6 +14,18 @@
 norm_eps = 1e-06
 rope_base = 1000000.0
 big_negative = -1e30
+
+
+def gather_by_bits(x, axis, dim):
+    ways, here, lap = (lax.axis_size(axis), lax.axis_index(axis), x.shape[dim])
+    line, have = (x, 1)
+    while have < ways:
+        line = jnp.concatenate(
+            [line, lax.ppermute(line, axis, [(d, (d - have) % ways) for d in range(ways)])],
+            axis=dim,
+        )
+        have = 2 * have
+    return jnp.roll(line, here * lap, axis=dim)
 
 
 def swapped(value, axis, stride):
@@ -118,9 +130,7 @@
     hidden = patch_rows.astype(jnp.float32) + branch_sum
     merged = layer_norm(hidden, merge_gain, merge_bias).astype(jnp.bfloat16).reshape(ICAP, 4 * VD)
     image_emb = jnp.dot(
-        merged,
-        lax.all_gather(merge_weight, "ctx", axis=0, tiled=True),
-        preferred_element_type=jnp.float32,
+        merged, gather_by_bits(merge_weight, "ctx", 0), preferred_element_type=jnp.float32
     ).astype(jnp.bfloat16)
     send_each = ICAP // shards
     slot_ids = jnp.arange(ICAP, dtype=jnp.int32)

time: 269 us -> 454 us (1.69)
  waiting for transfers between devices: 162 us -> 317 us
  local copies, waits for them, and re-layouts: 44.9 us -> 66.7 us
  starting transfers between devices: 6.82 us -> 16.6 us
    ppermute x0 -> x3, waiting for transfers between devices: none -> 260 us  [gather_by_bits(): lax.ppermute(line, axis, [(d, (d - have) % ways) for d in range(ways)])]
    all_gather x1 -> x0, waiting for transfers between devices: 115 us -> none  [local(): lax.all_gather(merge_weight, 'ctx', axis=0, tiled=True)]
    unnamed x33 -> x54, local copies, waits for them, and re-layouts: 4.95 us -> 21.6 us
    all_gather x1, waiting for transfers between devices: 3.11 us -> 17 us  [local(): full_rows = lax.all_gather(embeds, ('vis', 'tp'), axis=1, tiled=True)]
    ppermute x0 -> x3, starting transfers between devices: none -> 6.53 us  [gather_by_bits(): lax.ppermute(line, axis, [(d, (d - have) % ways) for d in range(ways)])]
    all_to_all x1, waiting for transfers between devices: 5.63 us -> 0.01 us  [local(): lax.all_to_all(outgoing.reshape(shards, send_each, slab_width), 'ctx', sp...]
    concatenate x0 -> x2, other arithmetic: none -> 5.31 us  [gather_by_bits(): jnp.concatenate([line, lax.ppermute(line, axis, [(d, (d - have) % ways) f...]
    concatenate x0 -> x1, local copies, waits for them, and re-layouts: none -> 5.3 us  [gather_by_bits(): return jnp.roll(line, here * lap, axis=dim)]
  transfers between devices with their start and end apart: 6 -> 8, of which waited for: 5 -> 6; matrix products, arithmetic and copies ran while one was open for 21% -> 15% of each run, Pallas kernels for 0% -> 0%
where the time goes in v1:
time: 454 us; the launch traced here: 453 us
  waiting for transfers between devices  317 us (70%)
  local copies, waits for them, and re-layouts  66.7 us (15%)
  matrix products  23.9 us (5%)
  starting transfers between devices  16.6 us (4%)
  other arithmetic  15.5 us (3%)
  between operations  13.5 us (3%)
    ppermute x3, waiting for transfers between devices, gather_by_bits(): lax.ppermute(line, axis, [(d, (d - have) % ways) for d in range(ways)])  260 us
    psum x1, waiting for transfers between devices, local(): branch_sum = lax.psum(branch_part, ('vis', 'tp'))  33.7 us
    unnamed x54, local copies, waits for them, and re-layouts  21.6 us
    all_gather x1, waiting for transfers between devices, local(): full_rows = lax.all_gather(embeds, ('vis', 'tp'), axis=1, tiled=True)  17 us
    reshape x1, local copies, waits for them, and re-layouts, local(): w_query.reshape(D, kv_heads * groups * HD)  14.4 us
    dot_general x1, local copies, waits for them, and re-layouts, local(): jnp.dot(normed_rows, w_query.reshape(D, kv_heads * groups * HD), preferre...  11.3 us
  transfers between devices with their start and end apart: 8, of which 6 were waited for; matrix products, arithmetic and copies ran while one was open for 15% of the time, Pallas kernels for 0%

profile of v1, /device:TPU:1, one launch (start us, length us, event | category | flops | bytes accessed | tf_op | source)
XLA Modules:
  0.0 453.1 jit_solution(987767087560467640)
XLA Ops:
  6.5 5.1 %collective-permute-start = (bf16[640,1024]{1,0:T(8,128)(2,1)}, bf16[640,1024]{1,0:T(8,128)(2,1)S(1)}, u32[]{:S(2)}, u32[]{:S(2)}) collective-permute-start(bf16[640,1024]{1,0:T(8,128)(2,1)} %param.24), channel_id=1, source_target_pairs={{0,14},{2,0},{4,2},{6,4},{8,6},{10,8},{12,10},{14,12},{1,15},{3,1}... | collective-permute-start | bytes 3932168 | tf_op jit(solution)/shard_map/ppermute | solution.py:24
  11.7 27.8 %collective-permute-done = bf16[640,1024]{1,0:T(8,128)(2,1)S(1)} collective-permute-done((bf16[640,1024]{1,0:T(8,128)(2,1)}, bf16[640,1024]{1,0:T(8,128)(2,1)S(1)}, u32[]{:S(2)}, u32[]{:S(2)}) %collective-permute-start) | collective-permute-done | bytes 1310752 | tf_op jit(solution)/shard_map/ppermute | solution.py:24
  39.5 2.1 pad_maximum_fusion.1
  43.2 55.3 %collective-permute-done.1 = bf16[1280,1024]{1,0:T(8,128)(2,1)S(1)} collective-permute-done((bf16[1280,1024]{1,0:T(8,128)(2,1)S(1)}, bf16[1280,1024]{1,0:T(8,128)(2,1)S(1)}, u32[]{:S(2)}, u32[]{:S(2)}) %collective-permute-start.1) | collective-permute-done | bytes 2621472 | tf_op jit(solution)/shard_map/ppermute | solution.py:24
  98.6 3.2 pad_maximum_fusion
  103.3 2.5 convolution_bitcast_fusion
  108.1 2.5 constant_dynamic-update-slice_fusion.7
  110.9 33.7 %all-reduce.2.cloned.1.call-done = f32[128,1280]{1,0:T(8,128)} async-done(((f32[128,1280]{1,0:T(8,128)}), f32[128,1280]{1,0:T(8,128)}) %all-reduce.2.cloned.1.call-update) | async-done | bytes 655376 | tf_op jit(solution)/shard_map/psum | solution.py:129
  149.8 3.5 constant_dynamic-update-slice_fusion.5
  153.4 176.4 %collective-permute-done.2 = bf16[2560,1024]{1,0:T(8,128)(2,1)} collective-permute-done((bf16[2560,1024]{1,0:T(8,128)(2,1)}, bf16[2560,1024]{1,0:T(8,128)(2,1)}, u32[]{:S(2)}, u32[]{:S(2)}) %collective-permute-start.2) | collective-permute-done | bytes 5242912 | tf_op jit(solution)/shard_map/ppermute | solution.py:24
  329.8 5.4 %constant_dynamic-update-slice_fusion.4 = bf16[10240,1024]{1,0:T(8,128)(2,1)} fusion(bf16[10240,1024]{1,0:T(8,128)(2,1)} %constant_dynamic-update-slice_fusion.5, bf16[2560,1024]{1,0:T(8,128)(2,1)} %collective-permute-done.2), kind=kLoop, calls=%fused_computation.106 | loop fusion | bytes 10485760
  339.3 5.3 %constant_dynamic-update-slice_fusion = bf16[10240,1024]{1,0:T(8,128)(2,1)} fusion(bf16[10240,1024]{1,0:T(8,128)(2,1)} %constant_dynamic-update-slice_fusion.1, bf16[2560,1024]{1,0:T(8,128)(2,1)} %collective-permute-done.2), kind=kLoop, calls=%fused_computation.102 | loop fusion | bytes 10485760 | tf_op jit(solution)/shard_map/jit(_roll_dynamic)/concatenate | solution.py:28
  344.6 6.9 %fusion.28 = bf16[32,1024]{1,0:T(8,128)(2,1)S(1)} fusion(bf16[32,5120]{1,0:T(8,128)(2,1)S(1)} %reshape.660, bf16[10240,1024]{1,0:T(8,128)(2,1)} %constant_dynamic-update-slice_fusion, s32[]{:T(128)S(6)} %select_n.320, s32[32]{0:T(128)S(1)} %multiply_add_fusion.1, pred[32]{0:T(512)(128)(4,1)S(1)} %get-tuple-element.54), kind=kOutput, calls=%fused_computation.34 | convolution fusion | flops 337709056 | bytes 10879140 | tf_op jit(solution)/shard_map/dot_general | solution.py:150
  352.2 6.7 %all-to-all-start = ((bf16[8,4,1024]{2,1,0:T(4,128)(2,1)}), bf16[8,4,1024]{2,1,0:T(4,128)(2,1)S(1)}, u32[]{:S(2)}, u32[]{:S(2)}) async-start(bf16[8,4,1024]{2,1,0:T(4,128)(2,1)} %reshape.661), calls=%async_computation | async-start | bytes 131072 | tf_op jit(solution)/shard_map/all_to_all | solution.py:151
  358.9 4.9 %copy.79 = bf16[512,8,4,128]{3,1,2,0:T(8,128)(2,1)} copy(bf16[512,8,4,128]{3,2,1,0:T(4,128)(2,1)} %bitcast.115) | data formatting | bytes 8388608
  363.8 6.5 %copy.63 = bf16[512,4096]{1,0:T(8,128)(2,1)} copy(bf16[512,4096]{0,1:T(8,128)(2,1)} %bitcast.113) | data formatting | bytes 8388608 | tf_op jit(solution)/shard_map/dot_general | solution.py:190
  373.0 17.0 %all-gather.3.cloned.1.call-done = bf16[128,4096]{1,0:T(8,128)(2,1)} async-done(((bf16[128,1024]{1,0:T(8,128)(2,1)}), bf16[128,4096]{1,0:T(8,128)(2,1)}) %all-gather.3.cloned.1.call-update) | async-done | bytes 1048592 | tf_op jit(solution)/shard_map/all_gather | solution.py:173
  391.5 3.8 fusion.36
  396.1 14.4 %reshape.663 = bf16[4096,1024]{1,0:T(8,128)(2,1)} reshape(bf16[4096,4,2,128]{3,2,1,0:T(2,128)(2,1)} %param.32) | data formatting | bytes 16777216 | tf_op jit(solution)/shard_map/reshape | solution.py:187
  410.5 11.3 %copy.64 = bf16[1024,4096]{1,0:T(8,128)(2,1)} copy(bf16[1024,4096]{0,1:T(8,128)(2,1)} %bitcast.112) | data formatting | bytes 16777216 | tf_op jit(solution)/shard_map/dot_general | solution.py:186
  421.7 4.5 gather_fusion
  426.3 6.5 %all-gather.5.cloned.1.call-done = bf16[1024,4,128]{0,2,1:T(8,128)(2,1)} async-done(((bf16[128,4,128]{0,2,1:T(8,128)(2,1)}), bf16[1024,4,128]{0,2,1:T(8,128)(2,1)}) %all-gather.5.cloned.1.call-update) | async-done | bytes 1048592 | tf_op jit(solution)/shard_map/all_gather | solution.py:201
  432.8 3.2 collective-permute-start.3
  436.3 5.9 %fusion.34 = f32[128,4,2,128]{0,3,2,1:T(8,128)S(1)} fusion(bf16[4,2,128,4096]{3,2,1,0:T(8,128)(2,1)} %bitcast.114, bf16[128,4096]{1,0:T(8,128)(2,1)S(1)} %copy-done.11, f32[4096]{0:T(1024)S(1)} %copy-done.20, f32[128]{0:T(128)S(1)} %add_rsqrt_fusion), kind=kOutput, calls=%fused_computation.38 | convolution fusion | flops 1075838976 | bytes 9978368 | tf_op jit(solution)/shard_map/dot_general | solution.py:186
  (121 shorter events, 25.1 us)
Async XLA Ops:
  6.5 95.5 %copy-start = (bf16[1280,3,4,80]{0,3,2,1:T(8,128)(2,1)S(1)}, bf16[1280,3,4,80]{0,3,2,1:T(8,128)(2,1)}, u32[]{:S(2)}) copy-start(bf16[1280,3,4,80]{0,3,2,1:T(8,128)(2,1)} %param.20) | copy-start | bytes 7372804
  6.5 36.3 %copy-start.10 = (bf16[128,1280]{1,0:T(8,128)(2,1)S(1)}, bf16[128,1280]{1,0:T(8,128)(2,1)}, u32[]{:S(2)}) copy-start(bf16[128,1280]{1,0:T(8,128)(2,1)} %param.17) | copy-start | bytes 983044
  6.5 138.1 %all-reduce.2.cloned.1.call-start = ((), (), s32[]{:S(2)}) async-start(), calls=%async_computation.1 | async-start | bytes 1310720 | tf_op jit(solution)/shard_map/psum | solution.py:129
  6.5 92.0 %copy-start.5 = (bf16[640,1024]{1,0:T(8,128)(2,1)S(1)}, bf16[640,1024]{1,0:T(8,128)(2,1)}, u32[]{:S(2)}) copy-start(bf16[640,1024]{1,0:T(8,128)(2,1)} %param.24) | copy-start | bytes 3932164
  6.5 32.9 %collective-permute-start = (bf16[640,1024]{1,0:T(8,128)(2,1)}, bf16[640,1024]{1,0:T(8,128)(2,1)S(1)}, u32[]{:S(2)}, u32[]{:S(2)}) collective-permute-start(bf16[640,1024]{1,0:T(8,128)(2,1)} %param.24), channel_id=1, source_target_pairs={{0,14},{2,0},{4,2},{6,4},{8,6},{10,8},{12,10},{14,12},{1,15},{3,1}... | collective-permute-start | bytes 3932168 | tf_op jit(solution)/shard_map/ppermute | solution.py:24
  39.5 62.3 %copy-start.7 = (bf16[640,1024]{1,0:T(8,128)(2,1)}, bf16[640,1024]{1,0:T(8,128)(2,1)S(1)}, u32[]{:S(2)}) copy-start(bf16[640,1024]{1,0:T(8,128)(2,1)S(1)} %collective-permute-done) | copy-start | bytes 3932164
  41.6 56.9 %collective-permute-start.1 = (bf16[1280,1024]{1,0:T(8,128)(2,1)S(1)}, bf16[1280,1024]{1,0:T(8,128)(2,1)S(1)}, u32[]{:S(2)}, u32[]{:S(2)}) collective-permute-start(bf16[1280,1024]{1,0:T(8,128)(2,1)S(1)} %pad_maximum_fusion.1), channel_id=1, source_target_pairs={{0,12},{2,14},{4,0},{6,2},{8,4},{10,6},{12,8},{14,10},{1,13},{3,15... | collective-permute-start | bytes 7864328 | tf_op jit(solution)/shard_map/ppermute | solution.py:24
  43.2 58.8 %copy-start.17 = (s32[128]{0:T(128)S(1)}, s32[128]{0:T(128)}, u32[]{:S(2)}) copy-start(s32[128]{0:T(128)} %param.26) | copy-start | bytes 1540
  43.2 58.9 %copy-start.21 = (f32[1280]{0:T(1024)S(1)}, f32[1280]{0:T(1024)}, u32[]{:S(2)}) copy-start(f32[1280]{0:T(1024)} %param.19) | copy-start | bytes 15364
  43.2 58.9 %copy-start.22 = (f32[1280]{0:T(1024)S(1)}, f32[1280]{0:T(1024)}, u32[]{:S(2)}) copy-start(f32[1280]{0:T(1024)} %param.18) | copy-start | bytes 15364
  101.8 228.0 %collective-permute-start.2 = (bf16[2560,1024]{1,0:T(8,128)(2,1)}, bf16[2560,1024]{1,0:T(8,128)(2,1)}, u32[]{:S(2)}, u32[]{:S(2)}) collective-permute-start(bf16[2560,1024]{1,0:T(8,128)(2,1)} %pad_maximum_fusion), channel_id=1, source_target_pairs={{0,8},{2,10},{4,12},{6,14},{8,0},{10,2},{12,4},{14,6},{1,9},{3,11}... | collective-permute-start | bytes 15728648 | tf_op jit(solution)/shard_map/ppermute | solution.py:24
  103.0 44.1 %copy-start.13 = (f32[1280]{0:T(1024)S(1)}, f32[1280]{0:T(1024)}, u32[]{:S(2)}) copy-start(f32[1280]{0:T(1024)} %param.23) | copy-start | bytes 15364
  103.0 44.1 %copy-start.14 = (f32[1280]{0:T(1024)S(1)}, f32[1280]{0:T(1024)}, u32[]{:S(2)}) copy-start(f32[1280]{0:T(1024)} %param.22) | copy-start | bytes 15364
  105.9 42.8 %copy-start.8 = (bf16[640,1024]{1,0:T(8,128)(2,1)S(1)}, bf16[640,1024]{1,0:T(8,128)(2,1)}, u32[]{:S(2)}) copy-start(bf16[640,1024]{1,0:T(8,128)(2,1)} %copy-done.7) | copy-start | bytes 3932164
  153.3 181.8 %copy-start.6 = (bf16[640,1024]{1,0:T(8,128)(2,1)S(1)}, bf16[640,1024]{1,0:T(8,128)(2,1)}, u32[]{:S(2)}) copy-start(bf16[640,1024]{1,0:T(8,128)(2,1)} %param.24) | copy-start | bytes 3932164
  153.4 183.0 %copy-start.9 = (bf16[640,1024]{1,0:T(8,128)(2,1)S(1)}, bf16[640,1024]{1,0:T(8,128)(2,1)}, u32[]{:S(2)}) copy-start(bf16[640,1024]{1,0:T(8,128)(2,1)} %copy-done.7) | copy-start | bytes 3932164
  352.2 18.1 %all-to-all-start = ((bf16[8,4,1024]{2,1,0:T(4,128)(2,1)}), bf16[8,4,1024]{2,1,0:T(4,128)(2,1)S(1)}, u32[]{:S(2)}, u32[]{:S(2)}) async-start(bf16[8,4,1024]{2,1,0:T(4,128)(2,1)} %reshape.661), calls=%async_computation | async-start | bytes 131072 | tf_op jit(solution)/shard_map/all_to_all | solution.py:151
  358.9 31.1 %all-gather.3.cloned.1.call-start = ((), (), s32[]{:S(2)}) async-start(), calls=%async_computation.2 | async-start | bytes 1310720 | tf_op jit(solution)/shard_map/all_gather | solution.py:173
  363.8 6.5 %copy-start.12 = (bf16[128,1024]{1,0:T(8,128)(2,1)S(1)}, bf16[128,1024]{1,0:T(8,128)(2,1)}, u32[]{:S(2)}) copy-start(bf16[128,1024]{1,0:T(8,128)(2,1)} %param.30) | copy-start | bytes 786436
  363.8 8.0 %copy-start.2 = (s32[1024]{0:T(1024)S(1)}, s32[1024]{0:T(1024)}, u32[]{:S(2)}) copy-start(s32[1024]{0:T(1024)} %param.29) | copy-start | bytes 12292
  363.8 27.7 %copy-start.20 = (f32[4096]{0:T(1024)S(1)}, f32[4096]{0:T(1024)}, u32[]{:S(2)}) copy-start(f32[4096]{0:T(1024)} %param.31) | copy-start | bytes 49156
  371.3 61.5 %all-gather.5.cloned.1.call-start = ((), (), s32[]{:S(2)}) async-start(), calls=%async_computation.3 | async-start | bytes 1179648 | tf_op jit(solution)/shard_map/all_gather | solution.py:201
  421.7 14.6 %copy-start.11 = (bf16[128,4096]{1,0:T(8,128)(2,1)S(1)}, bf16[128,4096]{1,0:T(8,128)(2,1)}, u32[]{:S(2)}) copy-start(bf16[128,4096]{1,0:T(8,128)(2,1)} %all-gather.3.cloned.1.call-done) | copy-start | bytes 3145732
  432.8 9.5 %collective-permute-start.3 = (bf16[1024,4,128]{0,2,1:T(8,128)(2,1)}, bf16[1024,4,128]{0,2,1:T(8,128)(2,1)S(1)}, u32[]{:S(2)}, u32[]{:S(2)}) collective-permute-start(bf16[1024,4,128]{0,2,1:T(8,128)(2,1)} %all-gather.5.cloned.1.call-done), channel_id=1, source_target_pairs={{0,1},{1,0},{2,3},{3,2},{4,5},{5,4},{6,7},{7,6},{8,9},{9,8},{10,11... | collective-permute-start | bytes 3145736 | tf_op jit(solution)/shard_map/ppermute | solution.py:32
  (7 other events, 28.2 us)
Sparse Core Ops, SparseCore 0:
  106.0 38.5 all-reduce.1
  371.4 18.5 all-gather.2
  396.2 36.5 all-gather.4
